TPU v7x, 512 devices: a whole 4x8x8 slice. The times are simulated.
512 devices in a mesh: blk: 64 (over y, z), mpo: 8 (over x, core).
Axes of the slice: x: 4, y: 8, z: 8, core: 2. Of those that a mesh axis runs over, the one named last changes fastest.
Arguments:
- wave: bfloat16 [6144, 128, 128], P('blk'), may hold values from -6 to 6
- left_env: bfloat16 [8, 64, 128, 128], P('mpo', 'blk'), may hold values from -0.5 to 0.5
- right_env: bfloat16 [8, 64, 128, 128], P('mpo', 'blk'), may hold values from -0.1875 to 0.1875
- right_sector: int32 [6144, 1], P('blk'), may hold values from 0 to 63; in each aligned block of 96 rows (0 to 95, 96 to 191, ...) at most 2 rows name the same one
- right_home: int32 [64], replicated, may hold values from 0 to 63, each once
Outputs:
- product: bfloat16 [6144, 128, 128], P('blk', None, 'mpo')
Inputs may be any that keep to these rules, and one draw needn't show every extreme that they name: `right_sector`: among the 96 blocks of one device (aligned blocks of rows) no right sector appears more than 2 times, and some sector appears exactly 2 times; every sector appears somewhere. `right_home`: each sector has its own storage row.
All inputs are finite; a program needn't handle non-finite values.
Results may differ from a plain program's by a relative error of at most 0.008.
Values may be sent and summed in bfloat16 or wider, within the bound.
No kernel may reach another device: no remote copies, remote signals or barrier semaphores. Data moves between devices by JAX's collectives and lax.ppermute only.
A program may use at most 64 MiB of HBM per device.

v0:
```python
import jax
import jax.numpy as jnp
from jax import lax
from jax.sharding import PartitionSpec as P


def local(wave, left_env, right_env, right_sector, right_home):
    blocks = wave.shape[0]
    sectors = left_env.shape[1]
    local_left = jnp.arange(blocks, dtype=jnp.int32) * sectors // blocks
    places = jnp.take(right_home, right_sector[:, 0], axis=0)
    chosen = jnp.take(left_env[0], local_left, axis=0)
    left = jnp.einsum("bik,bkj->bij", chosen, wave, preferred_element_type=jnp.float32).astype(
        jnp.bfloat16
    )
    every_right = lax.all_gather(right_env[0], "blk", axis=0, tiled=True)
    picked = jnp.take(every_right, places, axis=0)
    terms = jnp.einsum("bik,bjk->bij", left, picked, preferred_element_type=jnp.float32)
    summed = lax.psum_scatter(terms, "mpo", scatter_dimension=2, tiled=True)
    return summed.astype(jnp.bfloat16)


def solution(mesh):
    in_specs = (
        P("blk", None, None),
        P("mpo", "blk", None, None),
        P("mpo", "blk", None, None),
        P("blk", None),
        P(),
    )
    out_specs = P("blk", None, "mpo")
    return jax.shard_map(local, mesh=mesh, in_specs=in_specs, out_specs=out_specs, check_vma=False)
```

profile of v0, /device:TPU:1, one launch (start us, length us, event | category | flops | bytes accessed | tf_op | source)
XLA Modules:
  0.0 164.5 jit_solution(18109808292682006214)
XLA Ops:
  6.5 0.0 copy-start
  6.5 0.0 all-gather.3.cloned.1.call-start
  6.5 0.7 all-gather.3.cloned.1.call-update
  7.3 0.0 reduce-scatter.2.cloned.1.call-start
  7.3 0.8 fusion.17
  8.1 1.6 gather_fusion
  9.7 0.7 and_bitcast_fusion
  10.4 84.6 %all-gather.3.cloned.1.call-done = bf16[64,1,128,128]{3,2,1,0:T(8,128)(2,1)} async-done(((bf16[1,1,128,128]{3,2,1,0:T(8,128)(2,1)}), bf16[64,1,128,128]{3,2,1,0:T(8,128)(2,1)}) %all-gather.3.cloned.1.call-update) | async-done | bytes 2097168 | tf_op jit(solution)/shard_map/all_gather | solution.py:16
  95.0 0.0 copy-start.1
  95.0 4.3 %gather_fusion.1 = bf16[96,128,128]{2,1,0:T(8,128)(2,1)} fusion(bf16[64,128,128]{2,1,0:T(8,128)(2,1)} %bitcast.13, s32[1024]{0:T(1024)S(1)} %pad_clamp_fusion), kind=kCustom, calls=%fused_computation.1 | custom fusion | bytes 6291840 | tf_op jit(solution)/shard_map/jit(_take)/gather | solution.py:17
  99.4 0.0 copy-done
  99.4 0.0 copy-done.1
  99.4 7.8 %fusion = f32[96,128,128]{1,2,0:T(8,128)} fusion(bf16[96,128,128]{2,1,0:T(8,128)(2,1)} %gather_fusion.1, pred[96]{0:T(512)(128)(4,1)S(1)} %get-tuple-element.5, bf16[96,128,128]{2,1,0:T(8,128)(2,1)S(1)} %copy-done, pred[96]{0:T(512)(128)(4,1)S(1)} %compare_and_fusion, bf16[128,128]{1,0:T(8,128)(2,1)S(1)} %bitcast.15), kind=kOutput, calls=%fused_computation.2 | convolution fusion | flops 810024960 | bytes 12615872 | tf_op jit(solution)/shard_map/bik,bjk->bij/dot_general | solution.py:18
  107.2 0.0 reduce-scatter.2.cloned.1.call-update
  107.2 48.5 %reduce-scatter.2.cloned.1.call-done = f32[96,128,16]{1,2,0:T(8,128)} async-done(((f32[96,128,128]{1,2,0:T(8,128)}), f32[96,128,16]{1,2,0:T(8,128)}) %reduce-scatter.2.cloned.1.call-update) | async-done | bytes 786448 | tf_op jit(solution)/shard_map/reduce_scatter | solution.py:19
  155.7 1.9 %convert_element_type.7 = bf16[96,128,16]{1,2,0:T(8,128)(2,1)} convert(f32[96,128,16]{1,2,0:T(8,128)} %reduce-scatter.2.cloned.1.call-done) | non-fusion elementwise | flops 196608 | bytes 1179648 | tf_op jit(solution)/shard_map/convert_element_type | solution.py:20
  (3 shorter events, 0.0 us)
Async XLA Ops:
  6.5 92.9 %copy-start = (bf16[96,128,128]{2,1,0:T(8,128)(2,1)S(1)}, bf16[96,128,128]{2,1,0:T(8,128)(2,1)}, u32[]{:S(2)}) copy-start(bf16[96,128,128]{2,1,0:T(8,128)(2,1)} %param.5) | copy-start | bytes 9437188
  6.5 88.5 %all-gather.3.cloned.1.call-start = ((), (), s32[]{:S(2)}) async-start(), calls=%async_computation.2 | async-start | bytes 2129920 | tf_op jit(solution)/shard_map/all_gather | solution.py:16
  7.3 148.5 %reduce-scatter.2.cloned.1.call-start = ((), (), s32[]{:S(2)}) async-start(), calls=%async_computation.1 | async-start | bytes 7077888 | tf_op jit(solution)/shard_map/reduce_scatter | solution.py:19
  95.0 4.4 %copy-start.1 = (bf16[1,1,128,128]{3,2,1,0:T(8,128)(2,1)S(1)}, bf16[1,1,128,128]{3,2,1,0:T(8,128)(2,1)}, u32[]{:S(2)}) copy-start(bf16[1,1,128,128]{3,2,1,0:T(8,128)(2,1)} %param.6) | copy-start | bytes 98308
Sparse Core Ops, SparseCore 0:
  10.3 84.6 all-gather.2
  107.3 48.3 reduce-scatter.1
where the time goes:
time: 165 us
  waiting for transfers between devices  134 us (81%)
  between operations  13.4 us (8%)
  matrix products  7.78 us (5%)
  local copies, waits for them, and re-layouts  5.94 us (4%)
  other arithmetic  3.45 us (2%)
    all_gather x1, waiting for transfers between devices, local(): every_right = lax.all_gather(right_env[0], 'blk', axis=0, tiled=True)  84.6 us
    reduce_scatter x1, waiting for transfers between devices, local(): summed = lax.psum_scatter(terms, 'mpo', scatter_dimension=2, tiled=True)  48.5 us
    dot_general x1, matrix products, local(): jnp.einsum('bik,bjk->bij', left, picked, preferred_element_type=jnp.float32)  7.78 us
    gather x1, local copies, waits for them, and re-layouts, local(): picked = jnp.take(every_right, places, axis=0)  4.35 us
  transfers between devices with their start and end apart: 2, of which 2 were waited for; matrix products, arithmetic and copies ran while one was open for 2% of the time, Pallas kernels for 0%

commit v1 on v0

--- a/solution.py
+++ b/solution.py
@@ -13,7 +13,9 @@
     left = jnp.einsum("bik,bkj->bij", chosen, wave, preferred_element_type=jnp.float32).astype(
         jnp.bfloat16
     )
-    every_right = lax.all_gather(right_env[0], "blk", axis=0, tiled=True)
+    every_right = jnp.concatenate(
+        lax.all_to_all(jnp.stack([right_env[0]] * lax.axis_size("blk")), "blk", 0, 0), axis=0
+    )
     picked = jnp.take(every_right, places, axis=0)
     terms = jnp.einsum("bik,bjk->bij", left, picked, preferred_element_type=jnp.float32)
     summed = lax.psum_scatter(terms, "mpo", scatter_dimension=2, tiled=True)

time: 165 us -> 147 us (0.89)
  waiting for transfers between devices: 134 us -> 97.8 us
  starting transfers between devices: 0.04 us -> 17.4 us
  local copies, waits for them, and re-layouts: 5.94 us -> 8.31 us
    all_gather x1 -> x0, waiting for transfers between devices: 84.6 us -> none  [local(): every_right = lax.all_gather(right_env[0], 'blk', axis=0, tiled=True)]
    all_to_all x0 -> x1, waiting for transfers between devices: none -> 46.9 us  [local(): lax.all_to_all(jnp.stack([right_env[0]] * lax.axis_size('blk')), 'blk', 0...]
    all_to_all x0 -> x1, starting transfers between devices: none -> 17.4 us  [local(): lax.all_to_all(jnp.stack([right_env[0]] * lax.axis_size('blk')), 'blk', 0...]
    another operation x0 -> x1, local copies, waits for them, and re-layouts: none -> 2.72 us  [local(): jnp.stack([right_env[0]] * lax.axis_size('blk'))]
    reduce_scatter x1, waiting for transfers between devices: 48.5 us -> 50.9 us  [local(): summed = lax.psum_scatter(terms, 'mpo', scatter_dimension=2, tiled=True)]
  transfers between devices with their start and end apart: 2 -> 2, of which waited for: 2 -> 2; matrix products, arithmetic and copies ran while one was open for 2% -> 1% of each run, Pallas kernels for 0% -> 0%
where the time goes in v1:
time: 147 us
  waiting for transfers between devices  97.8 us (67%)
  starting transfers between devices  17.4 us (12%)
  between operations  13.5 us (9%)
  local copies, waits for them, and re-layouts  8.31 us (6%)
  matrix products  7.77 us (5%)
  other arithmetic  1.97 us (1%)
    reduce_scatter x1, waiting for transfers between devices, local(): summed = lax.psum_scatter(terms, 'mpo', scatter_dimension=2, tiled=True)  50.9 us
    all_to_all x1, waiting for transfers between devices, local(): lax.all_to_all(jnp.stack([right_env[0]] * lax.axis_size('blk')), 'blk', 0...  46.9 us
    all_to_all x1, starting transfers between devices, local(): lax.all_to_all(jnp.stack([right_env[0]] * lax.axis_size('blk')), 'blk', 0...  17.4 us
    dot_general x1, matrix products, local(): jnp.einsum('bik,bjk->bij', left, picked, preferred_element_type=jnp.float32)  7.77 us
    gather x1, local copies, waits for them, and re-layouts, local(): picked = jnp.take(every_right, places, axis=0)  4.35 us
  transfers between devices with their start and end apart: 2, of which 2 were waited for; matrix products, arithmetic and copies ran while one was open for 1% of the time, Pallas kernels for 0%

profile of v1, /device:TPU:1, one launch (start us, length us, event | category | flops | bytes accessed | tf_op | source)
XLA Modules:
  0.0 146.8 jit_solution(1059834565302476337)
XLA Ops:
  6.5 0.0 copy-start
  6.5 0.0 copy-start.2
  6.5 0.0 copy-start.1
  6.5 2.7 %stack.3 = bf16[64,1,128,128]{3,2,1,0:T(8,128)(2,1)} broadcast(bf16[128,128]{1,0:T(8,128)(2,1)} %bitcast.14), dimensions={2,3} | broadcast | bytes 2129920 | tf_op jit(solution)/shard_map/stack | solution.py:17
  9.3 17.4 %all-to-all-start = ((bf16[64,1,128,128]{3,2,1,0:T(8,128)(2,1)}), bf16[64,1,128,128]{3,2,1,0:T(8,128)(2,1)}, u32[]{:S(2)}, u32[]{:S(2)}) async-start(bf16[64,1,128,128]{3,2,1,0:T(8,128)(2,1)} %stack.3), calls=%async_computation | async-start | bytes 4194304 | tf_op jit(solution)/shard_map/all_to_all | solution.py:17
  26.7 0.0 reduce-scatter.2.cloned.1.call-start
  26.7 0.0 copy-done.2
  26.7 0.0 copy-done.1
  26.8 1.2 gather_fusion
  28.0 46.9 %all-to-all-done = bf16[64,1,128,128]{3,2,1,0:T(8,128)(2,1)} async-done(((bf16[64,1,128,128]{3,2,1,0:T(8,128)(2,1)}), bf16[64,1,128,128]{3,2,1,0:T(8,128)(2,1)}, u32[]{:S(2)}, u32[]{:S(2)}) %all-to-all-start) | async-done | bytes 2097184 | tf_op jit(solution)/shard_map/all_to_all | solution.py:17
  75.0 0.0 copy-start.3
  75.0 4.3 %gather_fusion.1 = bf16[96,128,128]{2,1,0:T(8,128)(2,1)} fusion(bf16[64,128,128]{2,1,0:T(8,128)(2,1)} %bitcast.5, s32[1024]{0:T(1024)S(1)} %pad_clamp_fusion), kind=kCustom, calls=%fused_computation.1 | custom fusion | bytes 6291840 | tf_op jit(solution)/shard_map/jit(_take)/gather | solution.py:19
  79.3 0.0 copy-done
  79.3 0.0 copy-done.3
  79.3 7.8 %fusion = f32[96,128,128]{1,2,0:T(8,128)} fusion(bf16[96,128,128]{2,1,0:T(8,128)(2,1)} %gather_fusion.1, pred[96]{0:T(512)(128)(4,1)S(1)} %get-tuple-element.5, bf16[96,128,128]{2,1,0:T(8,128)(2,1)S(1)} %copy-done, pred[96]{0:T(512)(128)(4,1)S(1)} %compare_and_fusion, bf16[128,128]{1,0:T(8,128)(2,1)S(1)} %bitcast.16), kind=kOutput, calls=%fused_computation.2 | convolution fusion | flops 810024960 | bytes 12615872 | tf_op jit(solution)/shard_map/bik,bjk->bij/dot_general | solution.py:20
  87.1 0.0 reduce-scatter.2.cloned.1.call-update
  87.1 50.9 %reduce-scatter.2.cloned.1.call-done = f32[96,128,16]{1,2,0:T(8,128)} async-done(((f32[96,128,128]{1,2,0:T(8,128)}), f32[96,128,16]{1,2,0:T(8,128)}) %reduce-scatter.2.cloned.1.call-update) | async-done | bytes 786448 | tf_op jit(solution)/shard_map/reduce_scatter | solution.py:21
  138.0 1.9 %convert_element_type.7 = bf16[96,128,16]{1,2,0:T(8,128)(2,1)} convert(f32[96,128,16]{1,2,0:T(8,128)} %reduce-scatter.2.cloned.1.call-done) | non-fusion elementwise | flops 196608 | bytes 1179648 | tf_op jit(solution)/shard_map/convert_element_type | solution.py:22
  (5 shorter events, 0.0 us)
Async XLA Ops:
  6.5 72.8 %copy-start = (bf16[96,128,128]{2,1,0:T(8,128)(2,1)S(1)}, bf16[96,128,128]{2,1,0:T(8,128)(2,1)}, u32[]{:S(2)}) copy-start(bf16[96,128,128]{2,1,0:T(8,128)(2,1)} %param.5) | copy-start | bytes 9437188
  6.5 20.2 %copy-start.2 = (s32[96,1]{0,1:T(1,128)S(1)}, s32[96,1]{0,1:T(1,128)}, u32[]{:S(2)}) copy-start(s32[96,1]{0,1:T(1,128)} %param.8) | copy-start | bytes 1156
  6.5 20.2 %copy-start.1 = (s32[64]{0:T(128)S(1)}, s32[64]{0:T(128)}, u32[]{:S(2)}) copy-start(s32[64]{0:T(128)} %param.9) | copy-start | bytes 772
  9.3 65.7 %all-to-all-start = ((bf16[64,1,128,128]{3,2,1,0:T(8,128)(2,1)}), bf16[64,1,128,128]{3,2,1,0:T(8,128)(2,1)}, u32[]{:S(2)}, u32[]{:S(2)}) async-start(bf16[64,1,128,128]{3,2,1,0:T(8,128)(2,1)} %stack.3), calls=%async_computation | async-start | bytes 4194304 | tf_op jit(solution)/shard_map/all_to_all | solution.py:17
  26.7 111.3 %reduce-scatter.2.cloned.1.call-start = ((), (), s32[]{:S(2)}) async-start(), calls=%async_computation.2 | async-start | bytes 7077888 | tf_op jit(solution)/shard_map/reduce_scatter | solution.py:21
  75.0 4.4 %copy-start.3 = (bf16[1,1,128,128]{3,2,1,0:T(8,128)(2,1)S(1)}, bf16[1,1,128,128]{3,2,1,0:T(8,128)(2,1)}, u32[]{:S(2)}) copy-start(bf16[1,1,128,128]{3,2,1,0:T(8,128)(2,1)} %param.6) | copy-start | bytes 98308
Sparse Core Ops, SparseCore 0:
  87.2 50.7 reduce-scatter.1
